TPU v7x, 256 devices: a whole 4x4x8 slice. The times are simulated.
256 devices in a mesh: run: 32 (over z, x_lo, core), entry: 8 (over x_hi, y).
Axes of the slice: x: 4 (x_hi: 2, x_lo: 2; x = x_hi * 2 + x_lo), y: 4, z: 8, core: 2. Of those that a mesh axis runs over, the one named last changes fastest.
Arguments:
- gradients: bfloat16 [16384, 65536], P('run', 'entry'), may hold values from -6 to 6
- probes: bfloat16 [65536, 512], P(('entry', 'run')), may hold values from -0.0234375 to 0.0234375
Outputs:
- projected: float32 [512, 65536], P('run', 'entry')
All inputs are finite; a program needn't handle non-finite values.
Results may differ from a plain program's by a relative error of at most 0.0026.
Values may be sent and summed in bfloat16 or wider, within the bound.
No kernel may reach another device: no remote copies, remote signals or barrier semaphores. Data moves between devices by JAX's collectives and lax.ppermute only.
A program may use at most 128 MiB of HBM per device.

v0:
```python
import jax
import jax.numpy as jnp
from jax import lax
from jax.sharding import PartitionSpec as P


def orthonormal(sketch, gram):
    factor = jnp.linalg.cholesky(gram)
    return lax.linalg.triangular_solve(
        factor, sketch, left_side=False, lower=True, transpose_a=True
    ).astype(jnp.bfloat16)


def per_device(gradients, probes):
    partial_sketch = jnp.dot(
        gradients,
        lax.all_gather(probes, "run", axis=0, tiled=True),
        preferred_element_type=jnp.float32,
    )
    sketch = lax.psum(partial_sketch, "entry")
    local_gram = jnp.dot(
        sketch.T, sketch, precision=lax.Precision.HIGHEST, preferred_element_type=jnp.float32
    )
    gram = lax.psum(local_gram, "run")
    basis = orthonormal(sketch, gram)
    return lax.psum_scatter(
        lax.dot_general(
            basis, gradients, (((0,), (0,)), ((), ())), preferred_element_type=jnp.float32
        ),
        "run",
        scatter_dimension=0,
        tiled=True,
    )


def solution(mesh):
    placed = (P("run", "entry"), P(("entry", "run"), None))
    return jax.shard_map(
        per_device, mesh=mesh, in_specs=placed, out_specs=P("run", "entry"), check_vma=False
    )
```

profile of v0, /device:TPU:8, one launch (start us, length us, event | category | flops | bytes accessed | tf_op | source)
XLA Modules:
  0.0 768.1 jit_solution(4741580711183889022)
XLA Ops:
  7.3 76.4 %all-gather.2.cloned.1.call-done = bf16[8192,512]{1,0:T(8,128)(2,1)} async-done(((bf16[256,512]{1,0:T(8,128)(2,1)}), bf16[8192,512]{1,0:T(8,128)(2,1)}) %all-gather.2.cloned.1.call-update) | async-done | bytes 8388624 | tf_op jit(solution)/shard_map/all_gather | solution.py:17
  83.7 11.3 %fusion.42 = f32[512,512]{1,0:T(8,128)} fusion(bf16[512,8192]{1,0:T(8,128)(2,1)} %param.2, bf16[8192,512]{1,0:T(8,128)(2,1)} %all-gather.2.cloned.1.call-done), kind=kOutput, calls=%fused_computation.78 | convolution fusion | flops 4294967296 | bytes 17825792 | tf_op jit(solution)/shard_map/dot_general | solution.py:15
  95.1 88.9 %all-reduce.4.cloned.1.call-done = f32[512,512]{1,0:T(8,128)} async-done(((f32[512,512]{1,0:T(8,128)}), f32[512,512]{1,0:T(8,128)}) %all-reduce.4.cloned.1.call-update) | async-done | bytes 1048592 | tf_op jit(solution)/shard_map/psum | solution.py:20
  184.0 4.5 fusion.43
  189.1 229.8 %all-reduce.6.cloned.1.call-done = f32[512,512]{0,1:T(8,128)} async-done(((f32[512,512]{0,1:T(8,128)}), f32[512,512]{0,1:T(8,128)}) %all-reduce.6.cloned.1.call-update) | async-done | bytes 1048592 | tf_op jit(solution)/shard_map/psum | solution.py:24
  418.9 1.6 copy.4
  420.5 1.4 fusion
  422.0 11.7 %cholesky.104 = f32[128,128]{1,0:T(8,128)S(1)} custom-call(f32[128,128]{1,0:T(8,128)S(1)} %cholesky.266), custom_call_target="Cholesky" | custom-call | tf_op jit(solution)/shard_map/jit(cholesky)/cholesky | solution.py:8
  433.7 9.8 %custom-call.30 = f32[1,128,128]{1,2,0:T(8,128)S(1)} custom-call(f32[1,128,128]{2,1,0:T(8,128)S(1)} %get-tuple-element.32), custom_call_target="InvertDiagBlocksLowerTriangular" | custom-call | tf_op jit(solution)/shard_map/jit(cholesky)/cholesky | solution.py:8
  444.3 11.7 %cholesky.217 = f32[128,128]{1,0:T(8,128)S(1)} custom-call(f32[128,128]{1,0:T(8,128)S(1)} %cholesky.270), custom_call_target="Cholesky" | custom-call | tf_op jit(solution)/shard_map/jit(cholesky)/cholesky | solution.py:8
  456.1 10.0 %custom-call.31 = f32[1,128,128]{1,2,0:T(8,128)S(1)} custom-call(f32[1,128,128]{2,1,0:T(8,128)S(1)} %get-tuple-element.29), custom_call_target="InvertDiagBlocksLowerTriangular" | custom-call | tf_op jit(solution)/shard_map/jit(cholesky)/cholesky | solution.py:8
  466.7 11.7 %cholesky.238 = f32[128,128]{1,0:T(8,128)S(1)} custom-call(f32[128,128]{1,0:T(8,128)S(1)} %cholesky.275), custom_call_target="Cholesky" | custom-call | tf_op jit(solution)/shard_map/jit(cholesky)/cholesky | solution.py:8
  479.2 9.8 %custom-call.32 = f32[1,128,128]{1,2,0:T(8,128)S(1)} custom-call(f32[1,128,128]{2,1,0:T(8,128)S(1)} %get-tuple-element.26), custom_call_target="InvertDiagBlocksLowerTriangular" | custom-call | tf_op jit(solution)/shard_map/jit(cholesky)/cholesky | solution.py:8
  489.6 11.7 %cholesky.255 = f32[128,128]{1,0:T(8,128)S(1)} custom-call(f32[128,128]{1,0:T(8,128)S(1)} %convolution_subtract_fusion.5), custom_call_target="Cholesky" | custom-call | tf_op jit(solution)/shard_map/jit(cholesky)/cholesky | solution.py:8
  505.6 10.6 %while.1 = (s32[]{:T(128)}, f32[512,512]{1,0:T(8,128)S(1)}, s32[4,2]{0,1:T(2,128)S(1)}, f32[4,128,128]{2,1,0:T(8,128)}, s32[]{:T(128)}) while((s32[]{:T(128)}, f32[512,512]{1,0:T(8,128)S(1)}, s32[4,2]{0,1:T(2,128)S(1)}, f32[4,128,128]{2,1,0:T(8,128)}, s32[]{:T(128)}) %tuple.30), condition=%wide.while_cond, body=%wide.while_body.sunk | while | flops 2 | bytes 132205 | solution.py:9
  506.2 2.0 bitcast_dynamic-update-slice_fusion.2
  508.9 2.0 bitcast_dynamic-update-slice_fusion.2
  511.5 2.0 bitcast_dynamic-update-slice_fusion.2
  514.2 2.0 bitcast_dynamic-update-slice_fusion.2
  516.1 40.1 %custom-call.33 = f32[4,128,128]{1,2,0:T(8,128)S(1)} custom-call(f32[4,128,128]{2,1,0:T(8,128)} %get-tuple-element.12), custom_call_target="InvertDiagBlocksLowerTriangular" | custom-call | tf_op jit(solution)/shard_map/triangular_solve | solution.py:9
  557.7 1.0 convolution_subtract_fusion
  559.1 1.5 convolution_subtract_fusion.2
  561.0 12.0 %fusion.9 = f32[512,8192]{1,0:T(8,128)} fusion(bf16[512,8192]{1,0:T(8,128)(2,1)} %param.2, bf16[512,128]{0,1:T(8,128)(2,1)S(1)} %convolution_convert_fusion, bf16[512,128]{0,1:T(8,128)(2,1)S(1)} %get-tuple-element.35, bf16[512,128]{0,1:T(8,128)(2,1)S(1)} %get-tuple-element.37, bf16[512,128]{0,1:T(8,128)(2,1)S(1)} %get-tuple-element.39), kind=kOutput, calls=%fused_computation.23 | convolution fusion | flops 4297064448 | bytes 25690112 | tf_op jit(solution)/shard_map/dot_general | solution.py:27
  573.1 188.2 %reduce-scatter.2.cloned.1.call-done = f32[16,8192]{1,0:T(8,128)} async-done(((f32[512,8192]{1,0:T(8,128)}), f32[16,8192]{1,0:T(8,128)}) %reduce-scatter.2.cloned.1.call-update) | async-done | bytes 524304 | tf_op jit(solution)/shard_map/reduce_scatter | solution.py:26
  (44 shorter events, 10.8 us)
Async XLA Ops:
  6.5 77.2 %all-gather.2.cloned.1.call-start = ((), (), s32[]{:S(2)}) async-start(), calls=%async_computation.1 | async-start | bytes 8650752 | tf_op jit(solution)/shard_map/all_gather | solution.py:17
  7.3 176.8 %all-reduce.4.cloned.1.call-start = ((), (), s32[]{:S(2)}) async-start(), calls=%async_computation.2 | async-start | bytes 2097152 | tf_op jit(solution)/shard_map/psum | solution.py:20
  95.1 323.9 %all-reduce.6.cloned.1.call-start = ((), (), s32[]{:S(2)}) async-start(), calls=%async_computation.3 | async-start | bytes 2097152 | tf_op jit(solution)/shard_map/psum | solution.py:24
  184.0 372.2 %copy-start = (f32[512,512]{1,0:T(8,128)S(1)}, f32[512,512]{1,0:T(8,128)}, u32[]{:S(2)}) copy-start(f32[512,512]{1,0:T(8,128)} %all-reduce.4.cloned.1.call-done) | copy-start | bytes 3145732
  188.6 572.7 %reduce-scatter.2.cloned.1.call-start = ((), (), s32[]{:S(2)}) async-start(), calls=%async_computation.4 | async-start | bytes 17301504 | tf_op jit(solution)/shard_map/reduce_scatter | solution.py:26
Sparse Core Ops, SparseCore 0:
  9.2 74.4 all-gather.1
  95.2 88.8 all-reduce.3
  188.7 230.2 all-reduce.5
  573.2 188.0 reduce-scatter.1
where the time goes:
time: 776 us; the launch traced here: 768 us
  waiting for transfers between devices  584 us (75%)
  other arithmetic  121 us (16%)
  matrix products  34.4 us (4%)
  between operations  16.1 us (2%)
  local copies, waits for them, and re-layouts  12.3 us (2%)
    psum x1, waiting for transfers between devices, per_device(): gram = lax.psum(local_gram, 'run')  230 us
    reduce_scatter x1, waiting for transfers between devices, per_device(): lax.psum_scatter(lax.dot_general(basis, gradients, (((0,), (0,)), ((), ()...  188 us
    psum x1, waiting for transfers between devices, per_device(): sketch = lax.psum(partial_sketch, 'entry')  88.9 us
    another operation x14, other arithmetic, orthonormal(): factor = jnp.linalg.cholesky(gram)  78.6 us
    all_gather x1, waiting for transfers between devices, per_device(): lax.all_gather(probes, 'run', axis=0, tiled=True)  76.4 us
    another operation x3, other arithmetic, orthonormal(): lax.linalg.triangular_solve(factor, sketch, left_side=False, lower=True,...  40.5 us
  transfers between devices with their start and end apart: 4, of which 4 were waited for; matrix products, arithmetic and copies ran while one was open for 0% of the time, Pallas kernels for 0%

commit v1 on v0

v1 whole, which is shorter than its diff:
```python
import functools

import jax
import jax.numpy as jnp
from jax import lax
from jax.sharding import PartitionSpec as P

HI = lax.Precision.HIGHEST
BLOCK = 128


def _swap(x, axis, size, bit):
    perm = [(i, i ^ (1 << bit)) for i in range(size)]
    return lax.ppermute(x, axis, perm)


def all_reduce(x, axis, size, bits):
    shape = x.shape
    x = x.reshape(-1)
    idx = lax.axis_index(axis)
    for bit in bits:
        mine = (idx >> bit) & 1
        halves = x.reshape(2, -1)
        keep = lax.dynamic_index_in_dim(halves, mine, 0, keepdims=False)
        send = lax.dynamic_index_in_dim(halves, 1 - mine, 0, keepdims=False)
        x = keep + _swap(send, axis, size, bit)
    for bit in reversed(bits):
        mine = (idx >> bit) & 1
        other = _swap(x, axis, size, bit)
        lo = jnp.where(mine == 0, x, other)
        hi = jnp.where(mine == 0, other, x)
        x = jnp.concatenate([lo, hi])
    return x.reshape(shape)


def inverse_factor(gram):
    n = gram.shape[0]
    nb = n // BLOCK
    eye = jnp.eye(BLOCK, dtype=gram.dtype)
    cols = []
    inv_diag = []
    for j in range(nb):
        s = j * BLOCK
        panel = gram[s:, s:s + BLOCK]
        if j > 0:
            left = jnp.concatenate([c[s - k * BLOCK:] for k, c in enumerate(cols)], axis=1)
            top = left[:BLOCK]
            panel = panel - jnp.dot(left, top.T, precision=HI)
        ljj = jnp.linalg.cholesky(panel[:BLOCK])
        ijj = lax.linalg.triangular_solve(ljj, eye, left_side=True, lower=True)
        if j < nb - 1:
            below = jnp.dot(panel[BLOCK:], ijj.T, precision=HI)
            cols.append(jnp.concatenate([ljj, below], axis=0))
        else:
            cols.append(ljj)
        inv_diag.append(ijj)

    def lblock(i, k):
        return cols[k][(i - k) * BLOCK:(i - k + 1) * BLOCK]

    inv = [[None] * nb for _ in range(nb)]
    for i in range(nb):
        inv[i][i] = inv_diag[i]
        for j in range(i - 1, -1, -1):
            acc = jnp.dot(lblock(i, j), inv[j][j], precision=HI)
            for k in range(j + 1, i):
                acc = acc + jnp.dot(lblock(i, k), inv[k][j], precision=HI)
            inv[i][j] = -jnp.dot(inv_diag[i], acc, precision=HI)
    zero = jnp.zeros((BLOCK, BLOCK), gram.dtype)
    rows = [jnp.concatenate([inv[i][j] if j <= i else zero for j in range(nb)], axis=1) for i in range(nb)]
    return jnp.concatenate(rows, axis=0)


def per_device(runs, entries, gradients, probes):
    run_bits = list(range(runs.bit_length() - 1))
    partial_sketch = jnp.dot(
        gradients,
        lax.all_gather(probes, "run", axis=0, tiled=True),
        preferred_element_type=jnp.float32,
    )
    sketch = all_reduce(partial_sketch, "entry", entries, list(range(entries.bit_length() - 1)))
    local_gram = jnp.dot(
        sketch.T, sketch, precision=HI, preferred_element_type=jnp.float32
    )
    gram = all_reduce(local_gram, "run", runs, run_bits)
    inv = inverse_factor(gram)
    basis = jnp.dot(sketch, inv.T, precision=HI).astype(jnp.bfloat16)
    return lax.psum_scatter(
        lax.dot_general(
            basis, gradients, (((0,), (0,)), ((), ())), preferred_element_type=jnp.float32
        ),
        "run",
        scatter_dimension=0,
        tiled=True,
    )


def solution(mesh):
    placed = (P("run", "entry"), P(("entry", "run"), None))
    body = functools.partial(per_device, mesh.shape["run"], mesh.shape["entry"])
    return jax.shard_map(
        body, mesh=mesh, in_specs=placed, out_specs=P("run", "entry"), check_vma=False
    )
```

time: 776 us -> 533 us (0.69)
  waiting for transfers between devices: 584 us -> 350 us
  other arithmetic: 121 us -> 92.5 us
  starting transfers between devices: 0.59 us -> 26.8 us
    psum x2 -> x0, waiting for transfers between devices: 319 us -> none  [the longest x1 230 us: per_device(): gram = lax.psum(local_gram, 'run')]
    ppermute x0 -> x16, waiting for transfers between devices: none -> 85.5 us  [_swap(): return lax.ppermute(x, axis, perm)]
    another operation x17 -> x20, other arithmetic: 119 us -> 91.8 us  [the longest x12 49.8 us: inverse_factor(): ljj = jnp.linalg.cholesky(panel[:BLOCK])]
    ppermute x0 -> x16, starting transfers between devices: none -> 26.8 us  [_swap(): return lax.ppermute(x, axis, perm)]
    another operation x17 -> x6, local copies, waits for them, and re-layouts: 10.7 us -> 2.05 us  [the longest x2 1.78 us: all_reduce(): halves = x.reshape(2, -1)]
  transfers between devices with their start and end apart: 4 -> 18, of which waited for: 4 -> 18; matrix products, arithmetic and copies ran while one was open for 0% -> 0% of each run, Pallas kernels for 0% -> 0%
where the time goes in v1:
time: 533 us; the launch traced here: 524 us
  waiting for transfers between devices  350 us (66%)
  other arithmetic  92.5 us (17%)
  matrix products  32.5 us (6%)
  starting transfers between devices  26.8 us (5%)
  between operations  14.6 us (3%)
  local copies, waits for them, and re-layouts  7.67 us (1%)
    reduce_scatter x1, waiting for transfers between devices, per_device(): lax.psum_scatter(lax.dot_general(basis, gradients, (((0,), (0,)), ((), ()...  187 us
    ppermute x16, waiting for transfers between devices, _swap(): return lax.ppermute(x, axis, perm)  85.5 us
    all_gather x1, waiting for transfers between devices, per_device(): lax.all_gather(probes, 'run', axis=0, tiled=True)  76.4 us
    another operation x12, other arithmetic, inverse_factor(): ljj = jnp.linalg.cholesky(panel[:BLOCK])  49.8 us
    another operation x8, other arithmetic, inverse_factor(): ijj = lax.linalg.triangular_solve(ljj, eye, left_side=True, lower=True)  42 us
    ppermute x16, starting transfers between devices, _swap(): return lax.ppermute(x, axis, perm)  26.8 us
    dot_general x1, matrix products, per_device(): lax.dot_general(basis, gradients, (((0,), (0,)), ((), ())), preferred_ele...  11.5 us
  transfers between devices with their start and end apart: 18, of which 18 were waited for; matrix products, arithmetic and copies ran while one was open for 0% of the time, Pallas kernels for 0%

profile of v1, /device:TPU:8, one launch (start us, length us, event | category | flops | bytes accessed | tf_op | source)
XLA Modules:
  0.0 523.8 jit_solution(2035024938101726990)
XLA Ops:
  7.3 76.4 %all-gather.2.cloned.1.call-done = bf16[8192,512]{1,0:T(8,128)(2,1)} async-done(((bf16[256,512]{1,0:T(8,128)(2,1)}), bf16[8192,512]{1,0:T(8,128)(2,1)}) %all-gather.2.cloned.1.call-update) | async-done | bytes 8388624 | tf_op jit(solution)/shard_map/all_gather | solution.py:78
  83.7 9.4 %fusion.92 = f32[512,512]{1,0:T(8,128)S(1)} fusion(bf16[512,8192]{1,0:T(8,128)(2,1)} %param.5, bf16[8192,512]{1,0:T(8,128)(2,1)} %all-gather.2.cloned.1.call-done), kind=kOutput, calls=%fused_computation.158 | convolution fusion | flops 4294967296 | bytes 17825792 | tf_op jit(solution)/shard_map/dot_general | solution.py:76
  95.7 13.4 %collective-permute-done = f32[131072]{0:T(1024)S(1)} collective-permute-done((f32[131072]{0:T(1024)S(1)}, f32[131072]{0:T(1024)S(1)}, u32[]{:S(2)}, u32[]{:S(2)}) %collective-permute-start) | collective-permute-done | bytes 524320 | tf_op jit(solution)/shard_map/ppermute | solution.py:14
  112.2 7.0 %collective-permute-done.1 = f32[65536]{0:T(1024)S(1)} collective-permute-done((f32[65536]{0:T(1024)S(1)}, f32[65536]{0:T(1024)S(1)}, u32[]{:S(2)}, u32[]{:S(2)}) %collective-permute-start.1) | collective-permute-done | bytes 262176 | tf_op jit(solution)/shard_map/ppermute | solution.py:14
  135.0 6.5 %collective-permute-done.4 = f32[65536]{0:T(1024)S(1)} collective-permute-done((f32[65536]{0:T(1024)S(1)}, f32[65536]{0:T(1024)S(1)}, u32[]{:S(2)}, u32[]{:S(2)}) %collective-permute-start.4) | collective-permute-done | bytes 262176 | tf_op jit(solution)/shard_map/ppermute | solution.py:14
  142.6 9.3 %collective-permute-done.5 = f32[131072]{0:T(1024)S(1)} collective-permute-done((f32[131072]{0:T(1024)S(1)}, f32[131072]{0:T(1024)S(1)}, u32[]{:S(2)}, u32[]{:S(2)}) %collective-permute-start.5) | collective-permute-done | bytes 524320 | tf_op jit(solution)/shard_map/ppermute | solution.py:14
  160.3 7.0 %collective-permute-done.7 = f32[65536]{0:T(1024)S(1)} collective-permute-done((f32[65536]{0:T(1024)S(1)}, f32[65536]{0:T(1024)S(1)}, u32[]{:S(2)}, u32[]{:S(2)}) %collective-permute-start.7) | collective-permute-done | bytes 262176 | tf_op jit(solution)/shard_map/ppermute | solution.py:14
  168.6 4.2 collective-permute-done.8
  174.8 4.2 collective-permute-done.9
  182.7 4.3 collective-permute-done.10
  190.5 4.6 collective-permute-done.11
  196.0 4.7 collective-permute-done.12
  201.0 4.8 collective-permute-done.13
  207.4 5.0 collective-permute-done.14
  215.4 11.7 %cholesky.74 = f32[128,128]{1,0:T(8,128)S(1)} custom-call(f32[128,128]{1,0:T(8,128)S(1)} %fusion.65), custom_call_target="Cholesky" | custom-call | tf_op jit(solution)/shard_map/jit(cholesky)/cholesky | solution.py:49
  228.5 9.8 %custom-call.8 = f32[1,128,128]{1,2,0:T(8,128)S(1)} custom-call(f32[1,128,128]{2,1,0:T(8,128)S(1)} %fusion.50), custom_call_target="InvertDiagBlocksLowerTriangular" | custom-call | tf_op jit(solution)/shard_map/triangular_solve/custom-call.0 | solution.py:50
  239.4 11.7 %cholesky.85 = f32[128,128]{1,0:T(8,128)S(1)} custom-call(f32[128,128]{1,0:T(8,128)S(1)} %fusion.63), custom_call_target="Cholesky" | custom-call | tf_op jit(solution)/shard_map/jit(cholesky)/cholesky | solution.py:49
  252.5 10.0 %custom-call.9 = f32[1,128,128]{1,2,0:T(8,128)S(1)} custom-call(f32[1,128,128]{2,1,0:T(8,128)S(1)} %fusion.51), custom_call_target="InvertDiagBlocksLowerTriangular" | custom-call | tf_op jit(solution)/shard_map/triangular_solve/custom-call.0 | solution.py:50
  265.2 11.7 %cholesky.96 = f32[128,128]{1,0:T(8,128)S(1)} custom-call(f32[128,128]{1,0:T(8,128)S(1)} %fusion.61), custom_call_target="Cholesky" | custom-call | tf_op jit(solution)/shard_map/jit(cholesky)/cholesky | solution.py:49
  278.2 9.8 %custom-call.10 = f32[1,128,128]{1,2,0:T(8,128)S(1)} custom-call(f32[1,128,128]{2,1,0:T(8,128)S(1)} %fusion.52), custom_call_target="InvertDiagBlocksLowerTriangular" | custom-call | tf_op jit(solution)/shard_map/triangular_solve/custom-call.0 | solution.py:50
  291.1 12.0 %cholesky.107 = f32[128,128]{1,0:T(8,128)S(1)} custom-call(f32[128,128]{1,0:T(8,128)S(1)} %fusion.59), custom_call_target="Cholesky" | custom-call | tf_op jit(solution)/shard_map/jit(cholesky)/cholesky | solution.py:49
  304.4 9.8 %custom-call.11 = f32[1,128,128]{1,2,0:T(8,128)S(1)} custom-call(f32[1,128,128]{2,1,0:T(8,128)S(1)} %fusion.53), custom_call_target="InvertDiagBlocksLowerTriangular" | custom-call | tf_op jit(solution)/shard_map/triangular_solve/custom-call.0 | solution.py:50
  317.9 11.5 %fusion.95 = f32[512,8192]{1,0:T(8,128)} fusion(bf16[512,512]{1,0:T(8,128)(2,1)S(1)} %convolution_convert_fusion, bf16[512,8192]{1,0:T(8,128)(2,1)} %param.5), kind=kOutput, calls=%fused_computation.161 | convolution fusion | flops 4294967296 | bytes 25690112 | tf_op jit(solution)/shard_map/dot_general | solution.py:89
  329.5 187.0 %reduce-scatter.2.cloned.1.call-done = f32[16,8192]{1,0:T(8,128)} async-done(((f32[512,8192]{1,0:T(8,128)}), f32[16,8192]{1,0:T(8,128)}) %reduce-scatter.2.cloned.1.call-update) | async-done | bytes 524304 | tf_op jit(solution)/shard_map/reduce_scatter | solution.py:88
  (129 shorter events, 63.3 us)
Async XLA Ops:
  6.5 77.2 %all-gather.2.cloned.1.call-start = ((), (), s32[]{:S(2)}) async-start(), calls=%async_computation.1 | async-start | bytes 8650752 | tf_op jit(solution)/shard_map/all_gather | solution.py:78
  7.3 509.3 %reduce-scatter.2.cloned.1.call-start = ((), (), s32[]{:S(2)}) async-start(), calls=%async_computation.2 | async-start | bytes 17301504 | tf_op jit(solution)/shard_map/reduce_scatter | solution.py:88
  95.0 14.1 %collective-permute-start = (f32[131072]{0:T(1024)S(1)}, f32[131072]{0:T(1024)S(1)}, u32[]{:S(2)}, u32[]{:S(2)}) collective-permute-start(f32[131072]{0:T(1024)S(1)} %bitcast.94), channel_id=1, source_target_pairs={{0,1},{1,0},{2,3},{3,2},{4,5},{5,4},{6,7},{7,6},{8,9},{9,8},{10,11... | collective-permute-start | bytes 1572872 | tf_op jit(solution)/shard_map/ppermute | solution.py:14
  110.0 9.2 %collective-permute-start.1 = (f32[65536]{0:T(1024)S(1)}, f32[65536]{0:T(1024)S(1)}, u32[]{:S(2)}, u32[]{:S(2)}) collective-permute-start(f32[65536]{0:T(1024)S(1)} %bitcast.96), channel_id=1, source_target_pairs={{0,2},{1,3},{2,0},{3,1},{4,6},{5,7},{6,4},{7,5},{8,10},{9,11},{10,... | collective-permute-start | bytes 786440 | tf_op jit(solution)/shard_map/ppermute | solution.py:14
  119.6 6.6 %collective-permute-start.2 = (f32[32768]{0:T(1024)S(1)}, f32[32768]{0:T(1024)S(1)}, u32[]{:S(2)}, u32[]{:S(2)}) collective-permute-start(f32[32768]{0:T(1024)S(1)} %bitcast.101), channel_id=1, source_target_pairs={{0,4},{1,5},{2,6},{3,7},{4,0},{5,1},{6,2},{7,3},{8,12},{9,13},{10,... | collective-permute-start | bytes 393224 | tf_op jit(solution)/shard_map/ppermute | solution.py:14
  126.2 6.6 %collective-permute-start.3 = (f32[32768]{0:T(1024)S(1)}, f32[32768]{0:T(1024)S(1)}, u32[]{:S(2)}, u32[]{:S(2)}) collective-permute-start(f32[32768]{0:T(1024)S(1)} %add.117), channel_id=1, source_target_pairs={{0,4},{1,5},{2,6},{3,7},{4,0},{5,1},{6,2},{7,3},{8,12},{9,13},{10,... | collective-permute-start | bytes 393224 | tf_op jit(solution)/shard_map/ppermute | solution.py:14
  132.8 8.7 %collective-permute-start.4 = (f32[65536]{0:T(1024)S(1)}, f32[65536]{0:T(1024)S(1)}, u32[]{:S(2)}, u32[]{:S(2)}) collective-permute-start(f32[65536]{0:T(1024)S(1)} %pad_maximum_fusion.2), channel_id=1, source_target_pairs={{0,2},{1,3},{2,0},{3,1},{4,6},{5,7},{6,4},{7,5},{8,10},{9,11},{10,... | collective-permute-start | bytes 786440 | tf_op jit(solution)/shard_map/ppermute | solution.py:14
  141.6 10.4 %collective-permute-start.5 = (f32[131072]{0:T(1024)S(1)}, f32[131072]{0:T(1024)S(1)}, u32[]{:S(2)}, u32[]{:S(2)}) collective-permute-start(f32[131072]{0:T(1024)S(1)} %pad_maximum_fusion), channel_id=1, source_target_pairs={{0,1},{1,0},{2,3},{3,2},{4,5},{5,4},{6,7},{7,6},{8,9},{9,8},{10,11... | collective-permute-start | bytes 1572872 | tf_op jit(solution)/shard_map/ppermute | solution.py:14
  156.0 2.0 collective-permute-start.6
  158.8 8.4 %collective-permute-start.7 = (f32[65536]{0:T(1024)S(1)}, f32[65536]{0:T(1024)S(1)}, u32[]{:S(2)}, u32[]{:S(2)}) collective-permute-start(f32[65536]{0:T(1024)S(1)} %bitcast.97), channel_id=1, source_target_pairs={{0,16},{8,24},{16,0},{24,8},{32,48},{40,56},{48,32},{56,40},{64,80... | collective-permute-start | bytes 786440 | tf_op jit(solution)/shard_map/ppermute | solution.py:14
  167.7 5.1 collective-permute-start.8
  173.0 6.0 %collective-permute-start.9 = (f32[16384]{0:T(1024)S(1)}, f32[16384]{0:T(1024)S(1)}, u32[]{:S(2)}, u32[]{:S(2)}) collective-permute-start(f32[16384]{0:T(1024)S(1)} %bitcast.102), channel_id=1, source_target_pairs={{0,64},{8,72},{16,80},{24,88},{32,96},{40,104},{48,112},{56,120},{... | collective-permute-start | bytes 196616 | tf_op jit(solution)/shard_map/ppermute | solution.py:14
  179.1 7.9 %collective-permute-start.10 = (f32[8192]{0:T(1024)S(1)}, f32[8192]{0:T(1024)S(1)}, u32[]{:S(2)}, u32[]{:S(2)}) collective-permute-start(f32[8192]{0:T(1024)S(1)} %bitcast.103), channel_id=1, source_target_pairs={{0,128},{8,136},{16,144},{24,152},{32,160},{40,168},{48,176},{56,1... | collective-permute-start | bytes 98312 | tf_op jit(solution)/shard_map/ppermute | solution.py:14
  187.0 8.1 %collective-permute-start.11 = (f32[8192]{0:T(1024)S(1)}, f32[8192]{0:T(1024)S(1)}, u32[]{:S(2)}, u32[]{:S(2)}) collective-permute-start(f32[8192]{0:T(1024)S(1)} %add.132), channel_id=1, source_target_pairs={{0,128},{8,136},{16,144},{24,152},{32,160},{40,168},{48,176},{56,1... | collective-permute-start | bytes 98312 | tf_op jit(solution)/shard_map/ppermute | solution.py:14
  195.2 5.6 %collective-permute-start.12 = (f32[16384]{0:T(1024)S(1)}, f32[16384]{0:T(1024)S(1)}, u32[]{:S(2)}, u32[]{:S(2)}) collective-permute-start(f32[16384]{0:T(1024)S(1)} %pad_maximum_fusion.7), channel_id=1, source_target_pairs={{0,64},{8,72},{16,80},{24,88},{32,96},{40,104},{48,112},{56,120},{... | collective-permute-start | bytes 196616 | tf_op jit(solution)/shard_map/ppermute | solution.py:14
  200.8 5.1 collective-permute-start.13
  205.9 6.5 %collective-permute-start.14 = (f32[65536]{0:T(1024)S(1)}, f32[65536]{0:T(1024)S(1)}, u32[]{:S(2)}, u32[]{:S(2)}) collective-permute-start(f32[65536]{0:T(1024)S(1)} %pad_maximum_fusion.3), channel_id=1, source_target_pairs={{0,16},{8,24},{16,0},{24,8},{32,48},{40,56},{48,32},{56,40},{64,80... | collective-permute-start | bytes 786440 | tf_op jit(solution)/shard_map/ppermute | solution.py:14
  212.5 2.2 collective-permute-start.15
Sparse Core Ops, SparseCore 0:
  9.2 74.4 all-gather.1
  329.6 186.8 reduce-scatter.1

commit v2 on v1

--- a/solution.py
+++ b/solution.py
@@ -85,14 +85,45 @@
     gram = all_reduce(local_gram, "run", runs, run_bits)
     inv = inverse_factor(gram)
     basis = jnp.dot(sketch, inv.T, precision=HI).astype(jnp.bfloat16)
-    return lax.psum_scatter(
-        lax.dot_general(
-            basis, gradients, (((0,), (0,)), ((), ())), preferred_element_type=jnp.float32
-        ),
-        "run",
-        scatter_dimension=0,
-        tiled=True,
-    )
+    return reduce_scatter_projection(basis, gradients, runs)
+
+
+def reduce_scatter_projection(basis, gradients, runs):
+    nz = runs // 4
+    probes = basis.shape[1]
+    rows = probes // runs
+    idx = lax.axis_index("run")
+    core = idx % 2
+    xlo = (idx // 2) % 2
+    z = idx // 4
+    cols = basis.reshape(basis.shape[0], nz, 2, 2, rows)
+
+    def project(c):
+        b = lax.dynamic_index_in_dim(cols, c, 3, keepdims=False).reshape(basis.shape[0], -1)
+        out = lax.dot_general(b, gradients, (((0,), (0,)), ((), ())), preferred_element_type=jnp.float32)
+        return out.reshape(nz, 2, rows, gradients.shape[1])
+
+    sent = project(1 - core)
+    got = lax.ppermute(sent, "run", [(i, i ^ 1) for i in range(runs)])
+    own = project(core)
+    half = gradients.shape[1] // 2
+
+    def ring(lo, step_sign):
+        perm = [(i, (i + 4 * step_sign) % runs) for i in range(runs)]
+        acc = None
+        for s in range(nz - 1):
+            d = (z - step_sign * (1 + s)) % nz
+            part = (lax.dynamic_index_in_dim(own, d, 0, keepdims=False)[..., lo:lo + half]
+                    + lax.dynamic_index_in_dim(got, d, 0, keepdims=False)[..., lo:lo + half])
+            acc = lax.ppermute(part if acc is None else acc + part, "run", perm)
+        part = (lax.dynamic_index_in_dim(own, z, 0, keepdims=False)[..., lo:lo + half]
+                + lax.dynamic_index_in_dim(got, z, 0, keepdims=False)[..., lo:lo + half])
+        return acc + part
+
+    mine = jnp.concatenate([ring(0, 1), ring(half, -1)], axis=-1)
+    keep = lax.dynamic_index_in_dim(mine, xlo, 0, keepdims=False)
+    send = lax.dynamic_index_in_dim(mine, 1 - xlo, 0, keepdims=False)
+    return keep + lax.ppermute(send, "run", [(i, i ^ 2) for i in range(runs)])
 
 
 def solution(mesh):

time: 533 us -> 480 us (0.901)
  waiting for transfers between devices: 350 us -> 236 us
  starting transfers between devices: 26.8 us -> 50.9 us
  local copies, waits for them, and re-layouts: 7.67 us -> 29.2 us
  other arithmetic: 92.5 us -> 103 us
  matrix products: 32.5 us -> 39 us
    reduce_scatter x1 -> x0, waiting for transfers between devices: 187 us -> none  [per_device(): lax.psum_scatter(lax.dot_general(basis, gradients, (((0,), (0,)), ((), ()...]
    ppermute x0 -> x16, waiting for transfers between devices: none -> 72.6 us  [the longest x14 65.4 us: ring(): acc = lax.ppermute(part if acc is None else acc + part, 'run', perm)]
    ppermute x0 -> x16, starting transfers between devices: none -> 24.6 us  [the longest x14 22.1 us: ring(): acc = lax.ppermute(part if acc is None else acc + part, 'run', perm)]
    squeeze x0 -> x2, local copies, waits for them, and re-layouts: none -> 21.5 us  [the longest x1 10.9 us: ring(): lax.dynamic_index_in_dim(got, d, 0, keepdims=False)[..., lo:lo + half]]
    add x0 -> x16, other arithmetic: none -> 10.4 us  [the longest x12 4.97 us: ring(): acc = lax.ppermute(part if acc is None else acc + part, 'run', perm)]
    dot_general x1 -> x2, matrix products: 11.5 us -> 18 us  [project(): lax.dot_general(b, gradients, (((0,), (0,)), ((), ())), preferred_element...]
  transfers between devices with their start and end apart: 18 -> 33, of which waited for: 18 -> 27; matrix products, arithmetic and copies ran while one was open for 0% -> 6% of each run, Pallas kernels for 0% -> 0%
where the time goes in v2:
time: 480 us; the launch traced here: 473 us
  waiting for transfers between devices  236 us (49%)
  other arithmetic  103 us (21%)
  starting transfers between devices  50.9 us (11%)
  matrix products  39 us (8%)
  local copies, waits for them, and re-layouts  29.2 us (6%)
  between operations  15.1 us (3%)
    ppermute x16, waiting for transfers between devices, _swap(): return lax.ppermute(x, axis, perm)  86 us
    all_gather x1, waiting for transfers between devices, per_device(): lax.all_gather(probes, 'run', axis=0, tiled=True)  76.4 us
    ppermute x14, waiting for transfers between devices, ring(): acc = lax.ppermute(part if acc is None else acc + part, 'run', perm)  65.4 us
    another operation x12, other arithmetic, inverse_factor(): ljj = jnp.linalg.cholesky(panel[:BLOCK])  49.7 us
    another operation x8, other arithmetic, inverse_factor(): ijj = lax.linalg.triangular_solve(ljj, eye, left_side=True, lower=True)  42.2 us
    ppermute x16, starting transfers between devices, _swap(): return lax.ppermute(x, axis, perm)  26.4 us
    ppermute x14, starting transfers between devices, ring(): acc = lax.ppermute(part if acc is None else acc + part, 'run', perm)  22.1 us
    dot_general x2, matrix products, project(): lax.dot_general(b, gradients, (((0,), (0,)), ((), ())), preferred_element...  18 us
  transfers between devices with their start and end apart: 33, of which 27 were waited for; matrix products, arithmetic and copies ran while one was open for 6% of the time, Pallas kernels for 0%

profile of v2, /device:TPU:8, one launch (start us, length us, event | category | flops | bytes accessed | tf_op | source)
XLA Modules:
  0.0 473.0 jit_solution(11625821711860543407)
XLA Ops:
  7.3 76.4 %all-gather.2.cloned.1.call-done = bf16[8192,512]{1,0:T(8,128)(2,1)} async-done(((bf16[256,512]{1,0:T(8,128)(2,1)}), bf16[8192,512]{1,0:T(8,128)(2,1)}) %all-gather.2.cloned.1.call-update) | async-done | bytes 8388624 | tf_op jit(solution)/shard_map/all_gather | solution.py:78
  83.7 9.4 %fusion.121 = f32[512,512]{1,0:T(8,128)S(1)} fusion(bf16[512,8192]{1,0:T(8,128)(2,1)} %param.5, bf16[8192,512]{1,0:T(8,128)(2,1)} %all-gather.2.cloned.1.call-done), kind=kOutput, calls=%fused_computation.237 | convolution fusion | flops 4294967296 | bytes 17825792 | tf_op jit(solution)/shard_map/dot_general | solution.py:76
  95.7 13.4 %collective-permute-done = f32[131072]{0:T(1024)S(1)} collective-permute-done((f32[131072]{0:T(1024)S(1)}, f32[131072]{0:T(1024)S(1)}, u32[]{:S(2)}, u32[]{:S(2)}) %collective-permute-start) | collective-permute-done | bytes 524320 | tf_op jit(solution)/shard_map/ppermute | solution.py:14
  112.2 7.0 %collective-permute-done.1 = f32[65536]{0:T(1024)S(1)} collective-permute-done((f32[65536]{0:T(1024)S(1)}, f32[65536]{0:T(1024)S(1)}, u32[]{:S(2)}, u32[]{:S(2)}) %collective-permute-start.1) | collective-permute-done | bytes 262176 | tf_op jit(solution)/shard_map/ppermute | solution.py:14
  142.6 9.3 %collective-permute-done.5 = f32[131072]{0:T(1024)S(1)} collective-permute-done((f32[131072]{0:T(1024)S(1)}, f32[131072]{0:T(1024)S(1)}, u32[]{:S(2)}, u32[]{:S(2)}) %collective-permute-start.5) | collective-permute-done | bytes 524320 | tf_op jit(solution)/shard_map/ppermute | solution.py:14
  215.4 11.7 %cholesky.74 = f32[128,128]{1,0:T(8,128)S(1)} custom-call(f32[128,128]{1,0:T(8,128)S(1)} %fusion.92), custom_call_target="Cholesky" | custom-call | tf_op jit(solution)/shard_map/jit(cholesky)/cholesky | solution.py:49
  228.5 9.8 %custom-call.8 = f32[1,128,128]{1,2,0:T(8,128)S(1)} custom-call(f32[1,128,128]{2,1,0:T(8,128)S(1)} %fusion.77), custom_call_target="InvertDiagBlocksLowerTriangular" | custom-call | tf_op jit(solution)/shard_map/triangular_solve/custom-call.0 | solution.py:50
  239.4 11.7 %cholesky.85 = f32[128,128]{1,0:T(8,128)S(1)} custom-call(f32[128,128]{1,0:T(8,128)S(1)} %fusion.90), custom_call_target="Cholesky" | custom-call | tf_op jit(solution)/shard_map/jit(cholesky)/cholesky | solution.py:49
  252.5 10.2 %custom-call.9 = f32[1,128,128]{1,2,0:T(8,128)S(1)} custom-call(f32[1,128,128]{2,1,0:T(8,128)S(1)} %fusion.78), custom_call_target="InvertDiagBlocksLowerTriangular" | custom-call | tf_op jit(solution)/shard_map/triangular_solve/custom-call.0 | solution.py:50
  265.4 11.7 %cholesky.96 = f32[128,128]{1,0:T(8,128)S(1)} custom-call(f32[128,128]{1,0:T(8,128)S(1)} %fusion.88), custom_call_target="Cholesky" | custom-call | tf_op jit(solution)/shard_map/jit(cholesky)/cholesky | solution.py:49
  278.5 9.8 %custom-call.10 = f32[1,128,128]{1,2,0:T(8,128)S(1)} custom-call(f32[1,128,128]{2,1,0:T(8,128)S(1)} %fusion.79), custom_call_target="InvertDiagBlocksLowerTriangular" | custom-call | tf_op jit(solution)/shard_map/triangular_solve/custom-call.0 | solution.py:50
  291.3 11.9 %cholesky.107 = f32[128,128]{1,0:T(8,128)S(1)} custom-call(f32[128,128]{1,0:T(8,128)S(1)} %fusion.86), custom_call_target="Cholesky" | custom-call | tf_op jit(solution)/shard_map/jit(cholesky)/cholesky | solution.py:49
  304.5 9.8 %custom-call.11 = f32[1,128,128]{1,2,0:T(8,128)S(1)} custom-call(f32[1,128,128]{2,1,0:T(8,128)S(1)} %fusion.80), custom_call_target="InvertDiagBlocksLowerTriangular" | custom-call | tf_op jit(solution)/shard_map/triangular_solve/custom-call.0 | solution.py:50
  318.1 9.0 %fusion = f32[8,2,16,8192]{3,2,1,0:T(8,128)} fusion(bf16[512,8192]{1,0:T(8,128)(2,1)} %param.5, bf16[512,8,2,2,16]{0,4,3,2,1:T(8,128)(2,1)S(1)} %bitcast.178, s32[]{:T(128)S(6)} %select_n.342), kind=kOutput, calls=%fused_computation | convolution fusion | flops 2147483648 | bytes 17039364 | tf_op jit(solution)/shard_map/dot_general | solution.py:103
  327.6 9.0 %fusion.2 = f32[8,2,16,8192]{3,2,1,0:T(8,128)} fusion(bf16[512,8192]{1,0:T(8,128)(2,1)} %param.5, bf16[512,8,2,2,16]{0,4,3,2,1:T(8,128)(2,1)S(1)} %bitcast.179, s32[]{:T(128)S(6)} %select_n.338), kind=kOutput, calls=%fused_computation.2 | convolution fusion | flops 2147483648 | bytes 17039364 | tf_op jit(solution)/shard_map/dot_general | solution.py:103
  336.6 10.5 %dynamic-slice_bitcast_fusion.1 = (f32[2,16,8192]{2,1,0:T(8,128)}, f32[2,16,8192]{2,1,0:T(8,128)}, f32[2,16,8192]{2,1,0:T(8,128)}, f32[2,16,8192]{2,1,0:T(8,128)...) fusion(f32[8,2,16,8192]{3,2,1,0:T(8,128)} %fusion.2, ...), kind=kLoop, calls=%fused_computation.44 | loop fusion | bytes 31457340 | tf_op jit(solution)/shard_map/jit(dynamic_index_in_dim)/squeeze | solution.py:116
  347.1 10.9 %dynamic-slice_bitcast_fusion = (f32[2,16,8192]{2,1,0:T(8,128)}, f32[2,16,8192]{2,1,0:T(8,128)}, f32[2,16,8192]{2,1,0:T(8,128)}, f32[2,16,8192]{2,1,0:T(8,128)},...) fusion(f32[8,2,16,8192]{3,2,1,0:T(8,128)} %collective-permute-d, ...), kind=kLoop, calls=%fused_computation.43 | loop fusion | bytes 31457340 | tf_op jit(solution)/shard_map/jit(dynamic_index_in_dim)/squeeze | solution.py:117
  362.9 10.7 %collective-permute-done.24 = f32[2,16,4096]{2,1,0:T(8,128)S(1)} collective-permute-done((f32[2,16,4096]{2,1,0:T(8,128)S(1)}, f32[2,16,4096]{2,1,0:T(8,128)S(1)}, u32[]{:S(2)}, u32[]{:S(2)}) %collective-permute-start.24) | collective-permute-done | bytes 524320 | tf_op jit(solution)/shard_map/ppermute | solution.py:118
  378.7 9.6 %collective-permute-done.25 = f32[2,16,4096]{2,1,0:T(8,128)S(1)} collective-permute-done((f32[2,16,4096]{2,1,0:T(8,128)S(1)}, f32[2,16,4096]{2,1,0:T(8,128)S(1)}, u32[]{:S(2)}, u32[]{:S(2)}) %collective-permute-start.25) | collective-permute-done | bytes 524320 | tf_op jit(solution)/shard_map/ppermute | solution.py:118
  392.8 9.6 %collective-permute-done.26 = f32[2,16,4096]{2,1,0:T(8,128)S(1)} collective-permute-done((f32[2,16,4096]{2,1,0:T(8,128)S(1)}, f32[2,16,4096]{2,1,0:T(8,128)S(1)}, u32[]{:S(2)}, u32[]{:S(2)}) %collective-permute-start.26) | collective-permute-done | bytes 524320 | tf_op jit(solution)/shard_map/ppermute | solution.py:118
  406.5 8.8 %collective-permute-done.27 = f32[2,16,4096]{2,1,0:T(8,128)S(1)} collective-permute-done((f32[2,16,4096]{2,1,0:T(8,128)S(1)}, f32[2,16,4096]{2,1,0:T(8,128)S(1)}, u32[]{:S(2)}, u32[]{:S(2)}) %collective-permute-start.27) | collective-permute-done | bytes 524320 | tf_op jit(solution)/shard_map/ppermute | solution.py:118
  419.5 8.0 %collective-permute-done.28 = f32[2,16,4096]{2,1,0:T(8,128)S(1)} collective-permute-done((f32[2,16,4096]{2,1,0:T(8,128)S(1)}, f32[2,16,4096]{2,1,0:T(8,128)S(1)}, u32[]{:S(2)}, u32[]{:S(2)}) %collective-permute-start.28) | collective-permute-done | bytes 524320 | tf_op jit(solution)/shard_map/ppermute | solution.py:118
  431.6 8.0 %collective-permute-done.29 = f32[2,16,4096]{2,1,0:T(8,128)S(1)} collective-permute-done((f32[2,16,4096]{2,1,0:T(8,128)S(1)}, f32[2,16,4096]{2,1,0:T(8,128)S(1)}, u32[]{:S(2)}, u32[]{:S(2)}) %collective-permute-start.29) | collective-permute-done | bytes 524320 | tf_op jit(solution)/shard_map/ppermute | solution.py:118
  457.7 7.2 %collective-permute-done.31 = f32[16,8192]{1,0:T(8,128)S(1)} collective-permute-done((f32[16,8192]{1,0:T(8,128)S(1)}, f32[16,8192]{1,0:T(8,128)S(1)}, u32[]{:S(2)}, u32[]{:S(2)}) %collective-permute-start.31) | collective-permute-done | bytes 524320 | tf_op jit(solution)/shard_map/ppermute | solution.py:126
  (214 shorter events, 154.3 us)
Async XLA Ops:
  6.5 77.2 %all-gather.2.cloned.1.call-start = ((), (), s32[]{:S(2)}) async-start(), calls=%async_computation | async-start | bytes 8650752 | tf_op jit(solution)/shard_map/all_gather | solution.py:78
  95.0 14.1 %collective-permute-start = (f32[131072]{0:T(1024)S(1)}, f32[131072]{0:T(1024)S(1)}, u32[]{:S(2)}, u32[]{:S(2)}) collective-permute-start(f32[131072]{0:T(1024)S(1)} %bitcast.182), channel_id=1, source_target_pairs={{0,1},{1,0},{2,3},{3,2},{4,5},{5,4},{6,7},{7,6},{8,9},{9,8},{10,11... | collective-permute-start | bytes 1572872 | tf_op jit(solution)/shard_map/ppermute | solution.py:14
  110.0 9.2 %collective-permute-start.1 = (f32[65536]{0:T(1024)S(1)}, f32[65536]{0:T(1024)S(1)}, u32[]{:S(2)}, u32[]{:S(2)}) collective-permute-start(f32[65536]{0:T(1024)S(1)} %bitcast.184), channel_id=1, source_target_pairs={{0,2},{1,3},{2,0},{3,1},{4,6},{5,7},{6,4},{7,5},{8,10},{9,11},{10,... | collective-permute-start | bytes 786440 | tf_op jit(solution)/shard_map/ppermute | solution.py:14
  132.8 9.0 %collective-permute-start.4 = (f32[65536]{0:T(1024)S(1)}, f32[65536]{0:T(1024)S(1)}, u32[]{:S(2)}, u32[]{:S(2)}) collective-permute-start(f32[65536]{0:T(1024)S(1)} %pad_maximum_fusion.2), channel_id=1, source_target_pairs={{0,2},{1,3},{2,0},{3,1},{4,6},{5,7},{6,4},{7,5},{8,10},{9,11},{10,... | collective-permute-start | bytes 786440 | tf_op jit(solution)/shard_map/ppermute | solution.py:14
  141.9 10.1 %collective-permute-start.5 = (f32[131072]{0:T(1024)S(1)}, f32[131072]{0:T(1024)S(1)}, u32[]{:S(2)}, u32[]{:S(2)}) collective-permute-start(f32[131072]{0:T(1024)S(1)} %pad_maximum_fusion), channel_id=1, source_target_pairs={{0,1},{1,0},{2,3},{3,2},{4,5},{5,4},{6,7},{7,6},{8,9},{9,8},{10,11... | collective-permute-start | bytes 1572872 | tf_op jit(solution)/shard_map/ppermute | solution.py:14
  158.8 8.4 %collective-permute-start.7 = (f32[65536]{0:T(1024)S(1)}, f32[65536]{0:T(1024)S(1)}, u32[]{:S(2)}, u32[]{:S(2)}) collective-permute-start(f32[65536]{0:T(1024)S(1)} %bitcast.185), channel_id=1, source_target_pairs={{0,16},{8,24},{16,0},{24,8},{32,48},{40,56},{48,32},{56,40},{64,80... | collective-permute-start | bytes 786440 | tf_op jit(solution)/shard_map/ppermute | solution.py:14
  179.1 7.9 %collective-permute-start.10 = (f32[8192]{0:T(1024)S(1)}, f32[8192]{0:T(1024)S(1)}, u32[]{:S(2)}, u32[]{:S(2)}) collective-permute-start(f32[8192]{0:T(1024)S(1)} %bitcast.191), channel_id=1, source_target_pairs={{0,128},{8,136},{16,144},{24,152},{32,160},{40,168},{48,176},{56,1... | collective-permute-start | bytes 98312 | tf_op jit(solution)/shard_map/ppermute | solution.py:14
  187.0 8.1 %collective-permute-start.11 = (f32[8192]{0:T(1024)S(1)}, f32[8192]{0:T(1024)S(1)}, u32[]{:S(2)}, u32[]{:S(2)}) collective-permute-start(f32[8192]{0:T(1024)S(1)} %add.367), channel_id=1, source_target_pairs={{0,128},{8,136},{16,144},{24,152},{32,160},{40,168},{48,176},{56,1... | collective-permute-start | bytes 98312 | tf_op jit(solution)/shard_map/ppermute | solution.py:14
  327.0 20.1 %collective-permute-start.16 = (f32[8,2,16,8192]{3,2,1,0:T(8,128)}, f32[8,2,16,8192]{3,2,1,0:T(8,128)}, u32[]{:S(2)}, u32[]{:S(2)}) collective-permute-start(f32[8,2,16,8192]{3,2,1,0:T(8,128)} %fusion), channel_id=1, source_target_pairs={{0,8},{8,0},{16,24},{24,16},{32,40},{40,32},{48,56},{56,48},{64,72... | collective-permute-start | bytes 25165832 | tf_op jit(solution)/shard_map/ppermute | solution.py:107
  359.6 14.1 %collective-permute-start.24 = (f32[2,16,4096]{2,1,0:T(8,128)S(1)}, f32[2,16,4096]{2,1,0:T(8,128)S(1)}, u32[]{:S(2)}, u32[]{:S(2)}) collective-permute-start(f32[2,16,4096]{2,1,0:T(8,128)S(1)} %slice_add_fusion.7), channel_id=1, source_target_pairs={{0,224},{8,232},{16,240},{24,248},{32,0},{40,8},{48,16},{56,24},{6... | collective-permute-start | bytes 1572872 | tf_op jit(solution)/shard_map/ppermute | solution.py:118
  361.9 15.0 %collective-permute-start.17 = (f32[2,16,4096]{2,1,0:T(8,128)S(1)}, f32[2,16,4096]{2,1,0:T(8,128)S(1)}, u32[]{:S(2)}, u32[]{:S(2)}) collective-permute-start(f32[2,16,4096]{2,1,0:T(8,128)S(1)} %slice_add_fusion.15), channel_id=1, source_target_pairs={{0,32},{8,40},{16,48},{24,56},{32,64},{40,72},{48,80},{56,88},{64,... | collective-permute-start | bytes 1572872 | tf_op jit(solution)/shard_map/ppermute | solution.py:118
  375.1 13.2 %collective-permute-start.25 = (f32[2,16,4096]{2,1,0:T(8,128)S(1)}, f32[2,16,4096]{2,1,0:T(8,128)S(1)}, u32[]{:S(2)}, u32[]{:S(2)}) collective-permute-start(f32[2,16,4096]{2,1,0:T(8,128)S(1)} %fusion.38), channel_id=1, source_target_pairs={{0,224},{8,232},{16,240},{24,248},{32,0},{40,8},{48,16},{56,24},{6... | collective-permute-start | bytes 1572872 | tf_op jit(solution)/shard_map/ppermute | solution.py:118
  378.4 14.3 %collective-permute-start.18 = (f32[2,16,4096]{2,1,0:T(8,128)S(1)}, f32[2,16,4096]{2,1,0:T(8,128)S(1)}, u32[]{:S(2)}, u32[]{:S(2)}) collective-permute-start(f32[2,16,4096]{2,1,0:T(8,128)S(1)} %fusion.45), channel_id=1, source_target_pairs={{0,32},{8,40},{16,48},{24,56},{32,64},{40,72},{48,80},{56,88},{64,... | collective-permute-start | bytes 1572872 | tf_op jit(solution)/shard_map/ppermute | solution.py:118
  389.7 12.7 %collective-permute-start.26 = (f32[2,16,4096]{2,1,0:T(8,128)S(1)}, f32[2,16,4096]{2,1,0:T(8,128)S(1)}, u32[]{:S(2)}, u32[]{:S(2)}) collective-permute-start(f32[2,16,4096]{2,1,0:T(8,128)S(1)} %fusion.37), channel_id=1, source_target_pairs={{0,224},{8,232},{16,240},{24,248},{32,0},{40,8},{48,16},{56,24},{6... | collective-permute-start | bytes 1572872 | tf_op jit(solution)/shard_map/ppermute | solution.py:118
  392.7 13.5 %collective-permute-start.19 = (f32[2,16,4096]{2,1,0:T(8,128)S(1)}, f32[2,16,4096]{2,1,0:T(8,128)S(1)}, u32[]{:S(2)}, u32[]{:S(2)}) collective-permute-start(f32[2,16,4096]{2,1,0:T(8,128)S(1)} %fusion.44), channel_id=1, source_target_pairs={{0,32},{8,40},{16,48},{24,56},{32,64},{40,72},{48,80},{56,88},{64,... | collective-permute-start | bytes 1572872 | tf_op jit(solution)/shard_map/ppermute | solution.py:118
  402.5 12.7 %collective-permute-start.27 = (f32[2,16,4096]{2,1,0:T(8,128)S(1)}, f32[2,16,4096]{2,1,0:T(8,128)S(1)}, u32[]{:S(2)}, u32[]{:S(2)}) collective-permute-start(f32[2,16,4096]{2,1,0:T(8,128)S(1)} %fusion.36), channel_id=1, source_target_pairs={{0,224},{8,232},{16,240},{24,248},{32,0},{40,8},{48,16},{56,24},{6... | collective-permute-start | bytes 1572872 | tf_op jit(solution)/shard_map/ppermute | solution.py:118
  406.4 13.0 %collective-permute-start.20 = (f32[2,16,4096]{2,1,0:T(8,128)S(1)}, f32[2,16,4096]{2,1,0:T(8,128)S(1)}, u32[]{:S(2)}, u32[]{:S(2)}) collective-permute-start(f32[2,16,4096]{2,1,0:T(8,128)S(1)} %fusion.43), channel_id=1, source_target_pairs={{0,32},{8,40},{16,48},{24,56},{32,64},{40,72},{48,80},{56,88},{64,... | collective-permute-start | bytes 1572872 | tf_op jit(solution)/shard_map/ppermute | solution.py:118
  415.3 12.3 %collective-permute-start.28 = (f32[2,16,4096]{2,1,0:T(8,128)S(1)}, f32[2,16,4096]{2,1,0:T(8,128)S(1)}, u32[]{:S(2)}, u32[]{:S(2)}) collective-permute-start(f32[2,16,4096]{2,1,0:T(8,128)S(1)} %fusion.35), channel_id=1, source_target_pairs={{0,224},{8,232},{16,240},{24,248},{32,0},{40,8},{48,16},{56,24},{6... | collective-permute-start | bytes 1572872 | tf_op jit(solution)/shard_map/ppermute | solution.py:118
  419.4 12.0 %collective-permute-start.21 = (f32[2,16,4096]{2,1,0:T(8,128)S(1)}, f32[2,16,4096]{2,1,0:T(8,128)S(1)}, u32[]{:S(2)}, u32[]{:S(2)}) collective-permute-start(f32[2,16,4096]{2,1,0:T(8,128)S(1)} %fusion.42), channel_id=1, source_target_pairs={{0,32},{8,40},{16,48},{24,56},{32,64},{40,72},{48,80},{56,88},{64,... | collective-permute-start | bytes 1572872 | tf_op jit(solution)/shard_map/ppermute | solution.py:118
  427.6 12.0 %collective-permute-start.29 = (f32[2,16,4096]{2,1,0:T(8,128)S(1)}, f32[2,16,4096]{2,1,0:T(8,128)S(1)}, u32[]{:S(2)}, u32[]{:S(2)}) collective-permute-start(f32[2,16,4096]{2,1,0:T(8,128)S(1)} %fusion.34), channel_id=1, source_target_pairs={{0,224},{8,232},{16,240},{24,248},{32,0},{40,8},{48,16},{56,24},{6... | collective-permute-start | bytes 1572872 | tf_op jit(solution)/shard_map/ppermute | solution.py:118
  431.5 12.0 %collective-permute-start.22 = (f32[2,16,4096]{2,1,0:T(8,128)S(1)}, f32[2,16,4096]{2,1,0:T(8,128)S(1)}, u32[]{:S(2)}, u32[]{:S(2)}) collective-permute-start(f32[2,16,4096]{2,1,0:T(8,128)S(1)} %fusion.41), channel_id=1, source_target_pairs={{0,32},{8,40},{16,48},{24,56},{32,64},{40,72},{48,80},{56,88},{64,... | collective-permute-start | bytes 1572872 | tf_op jit(solution)/shard_map/ppermute | solution.py:118
  439.7 10.5 %collective-permute-start.30 = (f32[2,16,4096]{2,1,0:T(8,128)S(1)}, f32[2,16,4096]{2,1,0:T(8,128)}, u32[]{:S(2)}, u32[]{:S(2)}) collective-permute-start(f32[2,16,4096]{2,1,0:T(8,128)S(1)} %fusion.33), channel_id=1, source_target_pairs={{0,224},{8,232},{16,240},{24,248},{32,0},{40,8},{48,16},{56,24},{6... | collective-permute-start | bytes 1572872 | tf_op jit(solution)/shard_map/ppermute | solution.py:118
  443.6 10.6 %collective-permute-start.23 = (f32[2,16,4096]{2,1,0:T(8,128)S(1)}, f32[2,16,4096]{2,1,0:T(8,128)}, u32[]{:S(2)}, u32[]{:S(2)}) collective-permute-start(f32[2,16,4096]{2,1,0:T(8,128)S(1)} %fusion.40), channel_id=1, source_target_pairs={{0,32},{8,40},{16,48},{24,56},{32,64},{40,72},{48,80},{56,88},{64,... | collective-permute-start | bytes 1572872 | tf_op jit(solution)/shard_map/ppermute | solution.py:118
  455.6 9.3 %collective-permute-start.31 = (f32[16,8192]{1,0:T(8,128)S(1)}, f32[16,8192]{1,0:T(8,128)S(1)}, u32[]{:S(2)}, u32[]{:S(2)}) collective-permute-start(f32[16,8192]{1,0:T(8,128)S(1)} %fusion.28), channel_id=1, source_target_pairs={{0,16},{8,24},{16,0},{24,8},{32,48},{40,56},{48,32},{56,40},{64,80... | collective-permute-start | bytes 1572872 | tf_op jit(solution)/shard_map/ppermute | solution.py:126
  (27 other events, 954.7 us)
Sparse Core Ops, SparseCore 0:
  9.2 74.4 all-gather.1
